TPU v7x, 32 devices: a whole 2x2x4 slice. The times are simulated.
32 devices in a mesh: ep: 16 (over z, y, core), dp: 2 (over x).
Axes of the slice: x: 2, y: 2, z: 4, core: 2. Of those that a mesh axis runs over, the one named last changes fastest.
Arguments:
- moe_rows: bfloat16 [1024, 3584], P(('dp', 'ep')), parts along dimension 0, may hold values from -6 to 6
- routes: int32 [1024, 4], P(('dp', 'ep')), parts along dimension 0, may hold values from 0 to 7, all different within a row; in each aligned block of 32 rows (0 to 31, 32 to 63, ...) at most 32 rows name the same one
- route_weights: float32 [1024, 4], P(('dp', 'ep')), parts along dimension 0, may hold values from 0.05 to 0.5
- w_gate: bfloat16 [16, 3584, 512], P('ep'), may hold values from -0.09375 to 0.09375
- w_up: bfloat16 [16, 3584, 512], P('ep'), may hold values from -0.09375 to 0.09375
- w_down: bfloat16 [16, 512, 3584], P('ep'), may hold values from -0.1875 to 0.1875
- queries: bfloat16 [128, 64, 576], P(('dp', 'ep')), parts along dimension 0, may hold values from -45 to 45
- latent_cache: bfloat16 [128, 128, 576], P(('dp', 'ep')), parts along dimension 0, may hold values from -6 to 6
- lengths: int32 [128], P(('dp', 'ep')), parts along dimension 0, may hold values from 2 to 128, as said below
Outputs:
- moe_out: bfloat16 [1024, 3584], P(('dp', 'ep')), parts along dimension 0
- attn_out: bfloat16 [128, 64, 512], P(('dp', 'ep')), parts along dimension 0
There are 2 independent parts, one for each index of `dp`. A program takes and returns all parts, laid end to end along the dimension named above; an argument that names none is the same for every part. Nothing has to cross between parts.
Inputs may be any that keep to these rules, and one draw needn't show every extreme that they name: `routes`: each row names 4 different experts; in each aligned block of 32 rows (the rows of one device) no expert is named by more than 32 rows, a bound that some block reaches. `lengths`: some row of every part uses all 128 positions.
All inputs are finite; a program needn't handle non-finite values.
Results may differ from a plain program's by a relative error of at most 0.0085.
Values may be sent and summed in bfloat16 or wider, within the bound.
No kernel may reach another device: no remote copies, remote signals or barrier semaphores. Data moves between devices by JAX's collectives and lax.ppermute only.
A program may use at most 128 MiB of HBM per device.

v0:
```python
import jax
import jax.numpy as jnp
from jax import lax
from jax.sharding import PartitionSpec as P

LATENT = 512
score_scale = 192.0 ** (-0.5)


def attend(queries, latent_cache, lengths):
    scores = (
        jnp.einsum("rhc,rlc->rhl", queries, latent_cache, preferred_element_type=jnp.float32)
        * score_scale
    )
    in_range = (
        jnp.arange(latent_cache.shape[1], dtype=jnp.int32)[None, None, :] < lengths[:, None, None]
    )
    scores = jnp.where(in_range, scores, -1e30)
    highest = jnp.max(scores, axis=-1, keepdims=True)
    expo = jnp.where(in_range, jnp.exp(scores - highest), 0.0)
    probs = (expo / jnp.sum(expo, axis=-1, keepdims=True)).astype(jnp.bfloat16)
    return jnp.einsum(
        "rhl,rlc->rhc", probs, latent_cache[:, :, :LATENT], preferred_element_type=jnp.float32
    ).astype(jnp.bfloat16)


def shards(moe_rows, routes, route_weights, w_gate, w_up, w_down, queries, latent_cache, lengths):
    attn_out = attend(queries, latent_cache, lengths)
    rows_here, model_width = moe_rows.shape
    picks = routes.shape[1]
    devices = lax.axis_size("ep")
    experts = devices // 2
    capacity = min(rows_here, 2 * rows_here * picks // experts)
    flat_experts = routes.reshape(-1)
    matches = (flat_experts[:, None] == jnp.arange(experts, dtype=jnp.int32)[None, :]).astype(
        jnp.int32
    )
    before = jnp.cumsum(matches, axis=0) - matches
    slot_index = jnp.sum(before * matches, axis=1)
    target = flat_experts * capacity + slot_index
    source_rows = jnp.repeat(moe_rows, picks, axis=0)
    packed = jnp.zeros((experts * capacity, model_width), jnp.bfloat16).at[target].set(source_rows)
    packed = packed.reshape(experts, capacity, model_width)
    outgoing = jnp.repeat(packed, 2, axis=0)
    received = lax.all_to_all(outgoing, "ep", split_axis=0, concat_axis=0, tiled=True)
    senders = received.shape[0]
    item_count = received.shape[1]
    flat_rows = received.reshape(-1, model_width)
    gate_act = jnp.dot(flat_rows, w_gate[0], preferred_element_type=jnp.float32)
    up_act = jnp.dot(flat_rows, w_up[0], preferred_element_type=jnp.float32)
    hidden = (jax.nn.silu(gate_act) * up_act).astype(jnp.bfloat16)
    partial_out = jnp.dot(hidden, w_down[0], preferred_element_type=jnp.float32)
    returned = lax.all_to_all(
        partial_out.reshape(senders, item_count, model_width),
        "ep",
        split_axis=0,
        concat_axis=0,
        tiled=True,
    )
    expert_out = jnp.sum(returned.reshape(experts, 2, capacity, model_width), axis=1).astype(
        jnp.bfloat16
    )
    slot_out = expert_out.reshape(experts * capacity, model_width)[target]
    slot_out = slot_out.reshape(rows_here, picks, model_width)
    moe_out = jnp.einsum(
        "rk,rkd->rd", route_weights, slot_out, preferred_element_type=jnp.float32
    ).astype(jnp.bfloat16)
    return (moe_out, attn_out)


def solution(mesh):
    in_specs = (
        P(("dp", "ep"), None),
        P(("dp", "ep"), None),
        P(("dp", "ep"), None),
        P("ep", None, None),
        P("ep", None, None),
        P("ep", None, None),
        P(("dp", "ep"), None, None),
        P(("dp", "ep"), None, None),
        P(("dp", "ep")),
    )
    out_specs = (P(("dp", "ep"), None), P(("dp", "ep"), None, None))
    return jax.shard_map(shards, mesh=mesh, in_specs=in_specs, out_specs=out_specs, check_vma=False)
```

profile of v0, /device:TPU:13, one launch (start us, length us, event | category | flops | bytes accessed | tf_op | source)
XLA Modules:
  0.0 276.1 jit_solution(15898886306179961386)
XLA Ops:
  0.6 0.0 copy-start
  0.6 0.8 copy.15
  1.5 0.7 broadcast_multiply_fusion
  2.1 0.1 eq.15
  2.2 0.1 fusion.21
  2.3 0.2 reduce_window_sum.11
  2.5 0.2 select_reduce_fusion
  2.7 0.1 copy.14
  2.8 0.1 mul.34
  2.9 1.2 broadcast_in_dim.35
  4.1 0.2 reshape.98
  4.3 2.5 scatter_custom_fusion
  6.8 0.4 broadcast_in_dim.36
  7.1 0.0 copy-start.4
  7.2 87.6 %all_to_all.10 = bf16[16,32,3584]{2,1,0:T(8,128)(2,1)S(1)} all-to-all(bf16[16,32,3584]{2,1,0:T(8,128)(2,1)S(1)} %bitcast.41), channel_id=1, replica_groups=mesh['ep'=16,'dp'=2] {'ep'}, dimensions={0} | all-to-all | bytes 7340032 | tf_op jit(solution)/shard_map/all_to_all | solution.py:45
  94.8 0.0 copy-done.4
  94.8 0.0 copy-start.5
  94.8 2.0 fusion.5
  96.8 0.0 copy-done.5
  96.8 0.0 copy-start.1
  96.9 2.1 fusion.10
  99.0 0.0 copy-done.1
  99.0 5.1 %fusion.1 = f32[16,32,3584]{2,1,0:T(8,128)} fusion(bf16[16,32,512]{2,1,0:T(8,128)(2,1)S(1)} %bitcast.45, bf16[1,512,3584]{2,1,0:T(8,128)(2,1)S(1)} %copy-done.1), kind=kOutput, calls=%fused_computation.4 | convolution fusion | flops 1879048192 | bytes 11534336 | tf_op jit(solution)/shard_map/dot_general | solution.py:52
  104.1 0.0 copy-start.3
  104.1 0.0 copy-start.6
  104.1 0.0 copy-start.2
  104.1 5.4 %all-to-all-start.1 = ((f32[16,32,3584]{2,1,0:T(8,128)}), f32[16,32,3584]{2,1,0:T(8,128)}, u32[]{:S(2)}, u32[]{:S(2)}) async-start(f32[16,32,3584]{2,1,0:T(8,128)} %fusion.1), calls=%async_computation.1 | async-start | bytes 14680064 | tf_op jit(solution)/shard_map/all_to_all | solution.py:53
  109.5 0.0 copy-done.3
  109.5 0.1 copy.17
  109.6 0.0 copy-done.6
  109.6 0.1 iota_compare_fusion.1
  109.7 0.0 copy-done
  109.7 0.0 copy-done.2
  109.7 0.2 fusion.14
  110.0 0.2 fusion.25
  110.2 1.3 convolution_convert_fusion
  111.4 157.9 %all-to-all-done.1 = f32[16,32,3584]{2,1,0:T(8,128)} async-done(((f32[16,32,3584]{2,1,0:T(8,128)}), f32[16,32,3584]{2,1,0:T(8,128)}, u32[]{:S(2)}, u32[]{:S(2)}) %all-to-all-start.1) | async-done | bytes 7340064 | tf_op jit(solution)/shard_map/all_to_all | solution.py:53
  269.4 4.1 %bitcast_reduce_fusion = bf16[8,32,3584]{2,1,0:T(8,128)(2,1)S(1)} fusion(f32[16,32,3584]{2,1,0:T(8,128)} %all-to-all-done.1), kind=kLoop, calls=%fused_computation.3 | loop fusion | flops 917504 | bytes 9175040 | tf_op jit(solution)/shard_map/reduce_sum | solution.py:60
  273.5 1.1 gather_fusion
  274.6 0.2 reshape.85
  274.8 0.6 fusion.26
  275.4 0.7 copy.21
  (2 shorter events, 0.0 us)
Async XLA Ops:
  0.6 109.1 %copy-start = (bf16[4,64,576]{2,1,0:T(8,128)(2,1)S(1)}, bf16[4,64,576]{2,1,0:T(8,128)(2,1)}, u32[]{:S(2)}) copy-start(bf16[4,64,576]{2,1,0:T(8,128)(2,1)} %param.15) | copy-start | bytes 884740
  7.1 87.6 %copy-start.4 = (bf16[1,3584,512]{2,1,0:T(8,128)(2,1)S(1)}, bf16[1,3584,512]{2,1,0:T(8,128)(2,1)}, u32[]{:S(2)}) copy-start(bf16[1,3584,512]{2,1,0:T(8,128)(2,1)} %param.12) | copy-start | bytes 11010052
  94.8 2.1 copy-start.5
  96.8 2.2 copy-start.1
  104.1 5.4 %copy-start.3 = (f32[32,4]{0,1:T(4,128)S(1)}, f32[32,4]{0,1:T(4,128)}, u32[]{:S(2)}) copy-start(f32[32,4]{0,1:T(4,128)} %param.11) | copy-start | bytes 1540
  104.1 5.5 %copy-start.6 = (s32[4]{0:T(128)S(1)}, s32[4]{0:T(128)}, u32[]{:S(2)}) copy-start(s32[4]{0:T(128)} %param.17) | copy-start | bytes 52
  104.1 5.6 %copy-start.2 = (bf16[4,128,576]{1,2,0:T(8,128)(2,1)S(1)}, bf16[4,128,576]{1,2,0:T(8,128)(2,1)}, u32[]{:S(2)}) copy-start(bf16[4,128,576]{1,2,0:T(8,128)(2,1)} %param.16) | copy-start | bytes 1769476
  104.1 165.2 %all-to-all-start.1 = ((f32[16,32,3584]{2,1,0:T(8,128)}), f32[16,32,3584]{2,1,0:T(8,128)}, u32[]{:S(2)}, u32[]{:S(2)}) async-start(f32[16,32,3584]{2,1,0:T(8,128)} %fusion.1), calls=%async_computation.1 | async-start | bytes 14680064 | tf_op jit(solution)/shard_map/all_to_all | solution.py:53
where the time goes:
time: 276 us
  waiting for transfers between devices  158 us (57%)
  blocking collectives  87.6 us (32%)
  matrix products  11.5 us (4%)
  local copies, waits for them, and re-layouts  7.5 us (3%)
  other arithmetic  5.47 us (2%)
  starting transfers between devices  5.37 us (2%)
    all_to_all x1, waiting for transfers between devices, shards(): lax.all_to_all(partial_out.reshape(senders, item_count, model_width), 'ep...  158 us
    all_to_all x1, blocking collectives, shards(): lax.all_to_all(outgoing, 'ep', split_axis=0, concat_axis=0, tiled=True)  87.6 us
  transfers between devices with their start and end apart: 1, of which 1 were waited for; matrix products, arithmetic and copies ran while one was open for 1% of the time, Pallas kernels for 0%

commit v1 on v0

--- a/solution.py
+++ b/solution.py
@@ -42,7 +42,19 @@
     packed = jnp.zeros((experts * capacity, model_width), jnp.bfloat16).at[target].set(source_rows)
     packed = packed.reshape(experts, capacity, model_width)
     outgoing = jnp.repeat(packed, 2, axis=0)
-    received = lax.all_to_all(outgoing, "ep", split_axis=0, concat_axis=0, tiled=True)
+    ways, here = (lax.axis_size("ep"), lax.axis_index("ep"))
+    width = outgoing.shape[0] // ways
+    shape = list(outgoing.shape)
+    shape[0] = width
+    height = shape[0]
+    shape[0] = height * ways
+    full = jnp.zeros(shape, outgoing.dtype)
+    for mask in range(ways):
+        part = lax.dynamic_slice_in_dim(outgoing, (here ^ mask) * width, width, axis=0)
+        if mask:
+            part = lax.ppermute(part, "ep", [(d, d ^ mask) for d in range(ways)])
+        full = lax.dynamic_update_slice_in_dim(full, part, (here ^ mask) * height, axis=0)
+    received = full
     senders = received.shape[0]
     item_count = received.shape[1]
     flat_rows = received.reshape(-1, model_width)

time: 276 us -> 286 us (1.036)
  blocking collectives: 87.6 us -> 0 us
  waiting for transfers between devices: 158 us -> 235 us
  starting transfers between devices: 5.37 us -> 23.3 us
    all_to_all x1 -> x0, blocking collectives: 87.6 us -> none  [shards(): lax.all_to_all(outgoing, 'ep', split_axis=0, concat_axis=0, tiled=True)]
    ppermute x0 -> x15, waiting for transfers between devices: none -> 77.1 us  [shards(): part = lax.ppermute(part, 'ep', [(d, d ^ mask) for d in range(ways)])]
    ppermute x0 -> x15, starting transfers between devices: none -> 17 us  [shards(): part = lax.ppermute(part, 'ep', [(d, d ^ mask) for d in range(ways)])]
  transfers between devices with their start and end apart: 1 -> 16, of which waited for: 1 -> 12; matrix products, arithmetic and copies ran while one was open for 1% -> 1% of each run, Pallas kernels for 0% -> 0%
where the time goes in v1:
time: 286 us; the launch traced here: 285 us
  waiting for transfers between devices  235 us (82%)
  starting transfers between devices  23.3 us (8%)
  matrix products  11.4 us (4%)
  local copies, waits for them, and re-layouts  8.46 us (3%)
  other arithmetic  5.47 us (2%)
    all_to_all x1, waiting for transfers between devices, shards(): lax.all_to_all(partial_out.reshape(senders, item_count, model_width), 'ep...  158 us
    ppermute x15, waiting for transfers between devices, shards(): part = lax.ppermute(part, 'ep', [(d, d ^ mask) for d in range(ways)])  77.1 us
    ppermute x15, starting transfers between devices, shards(): part = lax.ppermute(part, 'ep', [(d, d ^ mask) for d in range(ways)])  17 us
    all_to_all x1, starting transfers between devices, shards(): lax.all_to_all(partial_out.reshape(senders, item_count, model_width), 'ep...  6.3 us
  transfers between devices with their start and end apart: 16, of which 12 were waited for; matrix products, arithmetic and copies ran while one was open for 1% of the time, Pallas kernels for 0%

profile of v1, /device:TPU:13, one launch (start us, length us, event | category | flops | bytes accessed | tf_op | source)
XLA Modules:
  0.0 285.2 jit_solution(14965492920136115958)
XLA Ops:
  0.7 0.8 copy.15
  1.5 0.7 broadcast_multiply_fusion
  2.2 0.1 eq.15
  2.4 0.2 reduce_window_sum.11
  2.6 0.2 select_reduce_fusion
  2.8 0.1 mul.34
  2.9 1.2 broadcast_in_dim.39
  4.1 0.2 reshape.98
  4.4 2.5 scatter_custom_fusion
  6.9 0.4 broadcast_in_dim.40
  7.3 0.3 broadcast_in_dim.37
  7.6 0.3 constant_dynamic-slice_fusion.14
  8.0 0.7 collective-permute-start
  8.7 0.2 collective-permute-start.1
  9.0 1.5 collective-permute-start.2
  10.5 0.2 collective-permute-start.3
  10.6 1.6 collective-permute-start.4
  12.3 3.6 %collective-permute-done.1 = bf16[1,32,3584]{2,1,0:T(8,128)(2,1)S(1)} collective-permute-done((bf16[1,32,3584]{2,1,0:T(8,128)(2,1)S(1)}, bf16[1,32,3584]{2,1,0:T(8,128)(2,1)S(1)}, u32[]{:S(2)}, u32[]{:S(2)}) %collective-permute-start.1) | collective-permute-done | bytes 229408 | tf_op jit(solution)/shard_map/ppermute | solution.py:55
  15.9 0.9 collective-permute-start.6
  16.8 4.5 %collective-permute-done.2 = bf16[1,32,3584]{2,1,0:T(8,128)(2,1)S(1)} collective-permute-done((bf16[1,32,3584]{2,1,0:T(8,128)(2,1)S(1)}, bf16[1,32,3584]{2,1,0:T(8,128)(2,1)S(1)}, u32[]{:S(2)}, u32[]{:S(2)}) %collective-permute-start.2) | collective-permute-done | bytes 229408 | tf_op jit(solution)/shard_map/ppermute | solution.py:55
  21.3 2.3 collective-permute-start.7
  23.6 0.2 collective-permute-start.8
  23.9 2.3 collective-permute-start.9
  26.2 9.1 %collective-permute-done.5 = bf16[1,32,3584]{2,1,0:T(8,128)(2,1)S(1)} collective-permute-done((bf16[1,32,3584]{2,1,0:T(8,128)(2,1)S(1)}, bf16[1,32,3584]{2,1,0:T(8,128)(2,1)S(1)}, u32[]{:S(2)}, u32[]{:S(2)}) %collective-permute-start.5) | collective-permute-done | bytes 229408 | tf_op jit(solution)/shard_map/ppermute | solution.py:55
  35.3 4.4 %collective-permute-start.10 = (bf16[1,32,3584]{2,1,0:T(8,128)(2,1)S(1)}, bf16[1,32,3584]{2,1,0:T(8,128)(2,1)S(1)}, u32[]{:S(2)}, u32[]{:S(2)}) collective-permute-start(bf16[1,32,3584]{2,1,0:T(8,128)(2,1)S(1)} %get-tuple-element.6), channel_id=1, source_target_pairs={{0,22},{2,20},{4,18},{6,16},{8,30},{10,28},{12,26},{14,24},{16,6},... | collective-permute-start | bytes 688136 | tf_op jit(solution)/shard_map/ppermute | solution.py:55
  39.7 0.5 collective-permute-done.6
  40.2 0.9 collective-permute-start.11
  41.1 1.8 collective-permute-start.12
  42.9 20.2 %collective-permute-done.8 = bf16[1,32,3584]{2,1,0:T(8,128)(2,1)S(1)} collective-permute-done((bf16[1,32,3584]{2,1,0:T(8,128)(2,1)S(1)}, bf16[1,32,3584]{2,1,0:T(8,128)(2,1)S(1)}, u32[]{:S(2)}, u32[]{:S(2)}) %collective-permute-start.8) | collective-permute-done | bytes 229408 | tf_op jit(solution)/shard_map/ppermute | solution.py:55
  63.2 4.9 %collective-permute-done.9 = bf16[1,32,3584]{2,1,0:T(8,128)(2,1)S(1)} collective-permute-done((bf16[1,32,3584]{2,1,0:T(8,128)(2,1)S(1)}, bf16[1,32,3584]{2,1,0:T(8,128)(2,1)S(1)}, u32[]{:S(2)}, u32[]{:S(2)}) %collective-permute-start.9) | collective-permute-done | bytes 229408 | tf_op jit(solution)/shard_map/ppermute | solution.py:55
  68.1 9.8 %collective-permute-done.10 = bf16[1,32,3584]{2,1,0:T(8,128)(2,1)S(1)} collective-permute-done((bf16[1,32,3584]{2,1,0:T(8,128)(2,1)S(1)}, bf16[1,32,3584]{2,1,0:T(8,128)(2,1)S(1)}, u32[]{:S(2)}, u32[]{:S(2)}) %collective-permute-start.10) | collective-permute-done | bytes 229408 | tf_op jit(solution)/shard_map/ppermute | solution.py:55
  77.9 9.8 %collective-permute-done.11 = bf16[1,32,3584]{2,1,0:T(8,128)(2,1)S(1)} collective-permute-done((bf16[1,32,3584]{2,1,0:T(8,128)(2,1)S(1)}, bf16[1,32,3584]{2,1,0:T(8,128)(2,1)S(1)}, u32[]{:S(2)}, u32[]{:S(2)}) %collective-permute-start.11) | collective-permute-done | bytes 229408 | tf_op jit(solution)/shard_map/ppermute | solution.py:55
  87.8 5.3 %collective-permute-done.12 = bf16[1,32,3584]{2,1,0:T(8,128)(2,1)S(1)} collective-permute-done((bf16[1,32,3584]{2,1,0:T(8,128)(2,1)S(1)}, bf16[1,32,3584]{2,1,0:T(8,128)(2,1)S(1)}, u32[]{:S(2)}, u32[]{:S(2)}) %collective-permute-start.12) | collective-permute-done | bytes 229408 | tf_op jit(solution)/shard_map/ppermute | solution.py:55
  93.1 4.5 %collective-permute-done.13 = bf16[1,32,3584]{2,1,0:T(8,128)(2,1)S(1)} collective-permute-done((bf16[1,32,3584]{2,1,0:T(8,128)(2,1)S(1)}, bf16[1,32,3584]{2,1,0:T(8,128)(2,1)S(1)}, u32[]{:S(2)}, u32[]{:S(2)}) %collective-permute-start.13) | collective-permute-done | bytes 229408 | tf_op jit(solution)/shard_map/ppermute | solution.py:55
  97.6 4.9 %collective-permute-done.14 = bf16[1,32,3584]{2,1,0:T(8,128)(2,1)S(1)} collective-permute-done((bf16[1,32,3584]{2,1,0:T(8,128)(2,1)S(1)}, bf16[1,32,3584]{2,1,0:T(8,128)(2,1)S(1)}, u32[]{:S(2)}, u32[]{:S(2)}) %collective-permute-start.14) | collective-permute-done | bytes 229408 | tf_op jit(solution)/shard_map/ppermute | solution.py:55
  102.5 2.1 fusion.5
  104.6 2.1 multiply_convert_fusion
  106.8 5.1 %fusion.1 = f32[16,32,3584]{2,1,0:T(8,128)} fusion(bf16[16,32,512]{2,1,0:T(8,128)(2,1)S(1)} %bitcast.43, bf16[1,512,3584]{2,1,0:T(8,128)(2,1)S(1)} %copy-done.1), kind=kOutput, calls=%fused_computation.4 | convolution fusion | flops 1879048192 | bytes 11534336 | tf_op jit(solution)/shard_map/dot_general | solution.py:64
  111.9 6.3 %all-to-all-start = ((f32[16,32,3584]{2,1,0:T(8,128)}), f32[16,32,3584]{2,1,0:T(8,128)}, u32[]{:S(2)}, u32[]{:S(2)}) async-start(f32[16,32,3584]{2,1,0:T(8,128)} %fusion.1), calls=%async_computation | async-start | bytes 14680064 | tf_op jit(solution)/shard_map/all_to_all | solution.py:65
  118.4 0.2 fusion.8
  118.6 0.2 fusion.19
  118.8 1.3 convolution_convert_fusion
  120.1 158.3 %all-to-all-done = f32[16,32,3584]{2,1,0:T(8,128)} async-done(((f32[16,32,3584]{2,1,0:T(8,128)}), f32[16,32,3584]{2,1,0:T(8,128)}, u32[]{:S(2)}, u32[]{:S(2)}) %all-to-all-start) | async-done | bytes 7340064 | tf_op jit(solution)/shard_map/all_to_all | solution.py:65
  278.4 4.1 %bitcast_reduce_fusion = bf16[8,32,3584]{2,1,0:T(8,128)(2,1)S(1)} fusion(f32[16,32,3584]{2,1,0:T(8,128)} %all-to-all-done), kind=kLoop, calls=%fused_computation.3 | loop fusion | flops 917504 | bytes 9175040 | tf_op jit(solution)/shard_map/reduce_sum | solution.py:72
  282.5 1.1 gather_fusion
  283.6 0.2 reshape.85
  283.9 0.6 fusion.20
  284.5 0.7 copy.21
  (42 shorter events, 0.7 us)
Async XLA Ops:
  0.6 117.7 %copy-start = (bf16[4,64,576]{2,1,0:T(8,128)(2,1)S(1)}, bf16[4,64,576]{2,1,0:T(8,128)(2,1)}, u32[]{:S(2)}) copy-start(bf16[4,64,576]{2,1,0:T(8,128)(2,1)} %param.15) | copy-start | bytes 884740
  8.0 94.5 %copy-start.4 = (bf16[1,3584,512]{2,1,0:T(8,128)(2,1)S(1)}, bf16[1,3584,512]{2,1,0:T(8,128)(2,1)}, u32[]{:S(2)}) copy-start(bf16[1,3584,512]{2,1,0:T(8,128)(2,1)} %param.12) | copy-start | bytes 11010052
  8.0 4.3 %collective-permute-start = (bf16[1,32,3584]{2,1,0:T(8,128)(2,1)S(1)}, bf16[1,32,3584]{2,1,0:T(8,128)(2,1)S(1)}, u32[]{:S(2)}, u32[]{:S(2)}) collective-permute-start(bf16[1,32,3584]{2,1,0:T(8,128)(2,1)S(1)} %get-tuple-element.16), channel_id=1, source_target_pairs={{0,2},{2,0},{4,6},{6,4},{8,10},{10,8},{12,14},{14,12},{16,18},{18,... | collective-permute-start | bytes 688136 | tf_op jit(solution)/shard_map/ppermute | solution.py:55
  8.7 7.2 %collective-permute-start.1 = (bf16[1,32,3584]{2,1,0:T(8,128)(2,1)S(1)}, bf16[1,32,3584]{2,1,0:T(8,128)(2,1)S(1)}, u32[]{:S(2)}, u32[]{:S(2)}) collective-permute-start(bf16[1,32,3584]{2,1,0:T(8,128)(2,1)S(1)} %get-tuple-element.15), channel_id=1, source_target_pairs={{0,4},{2,6},{4,0},{6,2},{8,12},{10,14},{12,8},{14,10},{16,20},{18,... | collective-permute-start | bytes 688136 | tf_op jit(solution)/shard_map/ppermute | solution.py:55
  9.0 12.3 %collective-permute-start.2 = (bf16[1,32,3584]{2,1,0:T(8,128)(2,1)S(1)}, bf16[1,32,3584]{2,1,0:T(8,128)(2,1)S(1)}, u32[]{:S(2)}, u32[]{:S(2)}) collective-permute-start(bf16[1,32,3584]{2,1,0:T(8,128)(2,1)S(1)} %get-tuple-element.14), channel_id=1, source_target_pairs={{0,6},{2,4},{4,2},{6,0},{8,14},{10,12},{12,10},{14,8},{16,22},{18,... | collective-permute-start | bytes 688136 | tf_op jit(solution)/shard_map/ppermute | solution.py:55
  10.5 13.2 %collective-permute-start.3 = (bf16[1,32,3584]{2,1,0:T(8,128)(2,1)S(1)}, bf16[1,32,3584]{2,1,0:T(8,128)(2,1)S(1)}, u32[]{:S(2)}, u32[]{:S(2)}) collective-permute-start(bf16[1,32,3584]{2,1,0:T(8,128)(2,1)S(1)} %get-tuple-element.13), channel_id=1, source_target_pairs={{0,8},{2,10},{4,12},{6,14},{8,0},{10,2},{12,4},{14,6},{16,24},{18,... | collective-permute-start | bytes 688136 | tf_op jit(solution)/shard_map/ppermute | solution.py:55
  10.6 13.3 %collective-permute-start.4 = (bf16[1,32,3584]{2,1,0:T(8,128)(2,1)S(1)}, bf16[1,32,3584]{2,1,0:T(8,128)(2,1)S(1)}, u32[]{:S(2)}, u32[]{:S(2)}) collective-permute-start(bf16[1,32,3584]{2,1,0:T(8,128)(2,1)S(1)} %get-tuple-element.12), channel_id=1, source_target_pairs={{0,10},{2,8},{4,14},{6,12},{8,2},{10,0},{12,6},{14,4},{16,26},{18,... | collective-permute-start | bytes 688136 | tf_op jit(solution)/shard_map/ppermute | solution.py:55
  12.3 23.1 %collective-permute-start.5 = (bf16[1,32,3584]{2,1,0:T(8,128)(2,1)S(1)}, bf16[1,32,3584]{2,1,0:T(8,128)(2,1)S(1)}, u32[]{:S(2)}, u32[]{:S(2)}) collective-permute-start(bf16[1,32,3584]{2,1,0:T(8,128)(2,1)S(1)} %get-tuple-element.11), channel_id=1, source_target_pairs={{0,12},{2,14},{4,8},{6,10},{8,4},{10,6},{12,0},{14,2},{16,28},{18,... | collective-permute-start | bytes 688136 | tf_op jit(solution)/shard_map/ppermute | solution.py:55
  15.9 24.3 %collective-permute-start.6 = (bf16[1,32,3584]{2,1,0:T(8,128)(2,1)S(1)}, bf16[1,32,3584]{2,1,0:T(8,128)(2,1)S(1)}, u32[]{:S(2)}, u32[]{:S(2)}) collective-permute-start(bf16[1,32,3584]{2,1,0:T(8,128)(2,1)S(1)} %get-tuple-element.10), channel_id=1, source_target_pairs={{0,14},{2,12},{4,10},{6,8},{8,6},{10,4},{12,2},{14,0},{16,30},{18,... | collective-permute-start | bytes 688136 | tf_op jit(solution)/shard_map/ppermute | solution.py:55
  21.3 19.8 %collective-permute-start.7 = (bf16[1,32,3584]{2,1,0:T(8,128)(2,1)S(1)}, bf16[1,32,3584]{2,1,0:T(8,128)(2,1)S(1)}, u32[]{:S(2)}, u32[]{:S(2)}) collective-permute-start(bf16[1,32,3584]{2,1,0:T(8,128)(2,1)S(1)} %get-tuple-element.9), channel_id=1, source_target_pairs={{0,16},{2,18},{4,20},{6,22},{8,24},{10,26},{12,28},{14,30},{16,0},... | collective-permute-start | bytes 688136 | tf_op jit(solution)/shard_map/ppermute | solution.py:55
  23.6 39.5 %collective-permute-start.8 = (bf16[1,32,3584]{2,1,0:T(8,128)(2,1)S(1)}, bf16[1,32,3584]{2,1,0:T(8,128)(2,1)S(1)}, u32[]{:S(2)}, u32[]{:S(2)}) collective-permute-start(bf16[1,32,3584]{2,1,0:T(8,128)(2,1)S(1)} %get-tuple-element.8), channel_id=1, source_target_pairs={{0,18},{2,16},{4,22},{6,20},{8,26},{10,24},{12,30},{14,28},{16,2},... | collective-permute-start | bytes 688136 | tf_op jit(solution)/shard_map/ppermute | solution.py:55
  23.9 44.2 %collective-permute-start.9 = (bf16[1,32,3584]{2,1,0:T(8,128)(2,1)S(1)}, bf16[1,32,3584]{2,1,0:T(8,128)(2,1)S(1)}, u32[]{:S(2)}, u32[]{:S(2)}) collective-permute-start(bf16[1,32,3584]{2,1,0:T(8,128)(2,1)S(1)} %get-tuple-element.7), channel_id=1, source_target_pairs={{0,20},{2,22},{4,16},{6,18},{8,28},{10,30},{12,24},{14,26},{16,4},... | collective-permute-start | bytes 688136 | tf_op jit(solution)/shard_map/ppermute | solution.py:55
  35.3 42.6 %collective-permute-start.10 = (bf16[1,32,3584]{2,1,0:T(8,128)(2,1)S(1)}, bf16[1,32,3584]{2,1,0:T(8,128)(2,1)S(1)}, u32[]{:S(2)}, u32[]{:S(2)}) collective-permute-start(bf16[1,32,3584]{2,1,0:T(8,128)(2,1)S(1)} %get-tuple-element.6), channel_id=1, source_target_pairs={{0,22},{2,20},{4,18},{6,16},{8,30},{10,28},{12,26},{14,24},{16,6},... | collective-permute-start | bytes 688136 | tf_op jit(solution)/shard_map/ppermute | solution.py:55
  40.2 47.5 %collective-permute-start.11 = (bf16[1,32,3584]{2,1,0:T(8,128)(2,1)S(1)}, bf16[1,32,3584]{2,1,0:T(8,128)(2,1)S(1)}, u32[]{:S(2)}, u32[]{:S(2)}) collective-permute-start(bf16[1,32,3584]{2,1,0:T(8,128)(2,1)S(1)} %get-tuple-element.5), channel_id=1, source_target_pairs={{0,24},{2,26},{4,28},{6,30},{8,16},{10,18},{12,20},{14,22},{16,8},... | collective-permute-start | bytes 688136 | tf_op jit(solution)/shard_map/ppermute | solution.py:55
  41.1 51.9 %collective-permute-start.12 = (bf16[1,32,3584]{2,1,0:T(8,128)(2,1)S(1)}, bf16[1,32,3584]{2,1,0:T(8,128)(2,1)S(1)}, u32[]{:S(2)}, u32[]{:S(2)}) collective-permute-start(bf16[1,32,3584]{2,1,0:T(8,128)(2,1)S(1)} %get-tuple-element.4), channel_id=1, source_target_pairs={{0,26},{2,24},{4,30},{6,28},{8,18},{10,16},{12,22},{14,20},{16,10}... | collective-permute-start | bytes 688136 | tf_op jit(solution)/shard_map/ppermute | solution.py:55
  63.2 34.4 %collective-permute-start.13 = (bf16[1,32,3584]{2,1,0:T(8,128)(2,1)S(1)}, bf16[1,32,3584]{2,1,0:T(8,128)(2,1)S(1)}, u32[]{:S(2)}, u32[]{:S(2)}) collective-permute-start(bf16[1,32,3584]{2,1,0:T(8,128)(2,1)S(1)} %get-tuple-element.3), channel_id=1, source_target_pairs={{0,28},{2,30},{4,24},{6,26},{8,20},{10,22},{12,16},{14,18},{16,12}... | collective-permute-start | bytes 688136 | tf_op jit(solution)/shard_map/ppermute | solution.py:55
  68.1 34.4 %collective-permute-start.14 = (bf16[1,32,3584]{2,1,0:T(8,128)(2,1)S(1)}, bf16[1,32,3584]{2,1,0:T(8,128)(2,1)S(1)}, u32[]{:S(2)}, u32[]{:S(2)}) collective-permute-start(bf16[1,32,3584]{2,1,0:T(8,128)(2,1)S(1)} %get-tuple-element.2), channel_id=1, source_target_pairs={{0,30},{2,28},{4,26},{6,24},{8,22},{10,20},{12,18},{14,16},{16,14}... | collective-permute-start | bytes 688136 | tf_op jit(solution)/shard_map/ppermute | solution.py:55
  102.5 2.1 copy-start.5
  104.6 2.2 copy-start.1
  111.9 6.3 %copy-start.3 = (f32[32,4]{0,1:T(4,128)S(1)}, f32[32,4]{0,1:T(4,128)}, u32[]{:S(2)}) copy-start(f32[32,4]{0,1:T(4,128)} %param.11) | copy-start | bytes 1540
  111.9 6.4 %copy-start.6 = (s32[4]{0:T(128)S(1)}, s32[4]{0:T(128)}, u32[]{:S(2)}) copy-start(s32[4]{0:T(128)} %param.17) | copy-start | bytes 52
  111.9 6.5 %copy-start.2 = (bf16[4,128,576]{1,2,0:T(8,128)(2,1)S(1)}, bf16[4,128,576]{1,2,0:T(8,128)(2,1)}, u32[]{:S(2)}) copy-start(bf16[4,128,576]{1,2,0:T(8,128)(2,1)} %param.16) | copy-start | bytes 1769476
  111.9 166.6 %all-to-all-start = ((f32[16,32,3584]{2,1,0:T(8,128)}), f32[16,32,3584]{2,1,0:T(8,128)}, u32[]{:S(2)}, u32[]{:S(2)}) async-start(f32[16,32,3584]{2,1,0:T(8,128)} %fusion.1), calls=%async_computation | async-start | bytes 14680064 | tf_op jit(solution)/shard_map/all_to_all | solution.py:65
